TPU v7x, 128 devices: a whole 4x4x4 slice. The times are simulated.
128 devices in a mesh: row: 16 (over x, y), col: 8 (over z, core).
Axes of the slice: x: 4, y: 4, z: 4, core: 2. Of those that a mesh axis runs over, the one named last changes fastest.
Arguments:
- pattern_in: int32 [64, 16], replicated, may hold values from 0 to 63, as said below
- pattern_mid: int32 [64, 16], replicated, may hold values from 0 to 63, as said below
- pattern_out: int32 [64, 16], replicated, may hold values from 0 to 63, as said below
- density_blocks: float32 [4, 16, 2, 8, 256, 256], P(None, 'row', None, 'col'), as said below
Outputs:
- purified_blocks: float32 [4, 16, 2, 8, 256, 256], P(None, 'row', None, 'col')
Inputs may be any that keep to these rules, and one draw needn't show every extreme that they name: `pattern_in`: slot l * 8 + c of block row I names a block column congruent to c modulo 8; no column stands twice in a row; slot I mod 8 of row I names I; J stands in row I exactly when I stands in row J. `pattern_mid`: as for pattern_in. `pattern_out`: as for pattern_in. `density_blocks`: the block of row J for column I is the transpose of the block of row I for column J.
All inputs are finite; a program needn't handle non-finite values.
Results may differ from a plain program's by a relative error of at most 0.0091.
Values may be sent and summed in bfloat16 or wider, within the bound.
No kernel may reach another device: no remote copies, remote signals or barrier semaphores. Data moves between devices by JAX's collectives and lax.ppermute only.
A program may use at most 128 MiB of HBM per device.

v0:
```python
import jax
import jax.numpy as jnp
from jax import lax
from jax.sharding import PartitionSpec as P

ITERS = 2


def purify_section(owned, cur_list, next_list, grid_rows, grid_cols, row_index, col_index):
    block_rows = owned.shape[0]
    slot_pairs = owned.shape[2]
    edge_size = owned.shape[4]
    total_rows = cur_list.shape[0]
    slot_count = cur_list.shape[1]
    occupied = total_rows * edge_size / 2.0
    panels = owned.astype(jnp.bfloat16)
    owned_slots = owned[:, 0, :, 0]
    my_rows = lax.dynamic_index_in_dim(
        cur_list.reshape(block_rows, grid_rows, slot_count), row_index, axis=1, keepdims=False
    )
    my_residue = lax.dynamic_index_in_dim(
        my_rows.reshape(block_rows, slot_pairs, grid_cols), col_index, axis=2, keepdims=False
    )
    own_index = jnp.arange(block_rows, dtype=jnp.int32) * grid_rows + row_index
    diag_term = jnp.sum(
        jnp.where(my_residue == own_index[:, None], jnp.trace(owned_slots, axis1=2, axis2=3), 0.0)
    )
    next_trace = None
    trace_now = lax.psum(diag_term, ("row", "col"))
    gathered_rows = lax.all_gather(panels, "col", axis=3, tiled=True).reshape(
        block_rows, slot_count, edge_size, edge_size
    )
    next_rows = lax.dynamic_index_in_dim(
        next_list.reshape(block_rows, grid_rows, slot_count), row_index, axis=1, keepdims=False
    )
    out_cols = lax.dynamic_index_in_dim(
        next_rows.reshape(block_rows, slot_pairs, grid_cols), col_index, axis=2, keepdims=False
    )
    inner_safe = jnp.maximum(my_rows, 0)
    valid_inner = my_rows >= 0
    valid_out = out_cols >= 0
    column_panels = lax.all_gather(panels, "row", axis=1, tiled=True).reshape(
        total_rows * slot_pairs, edge_size, edge_size
    )
    residue_lists = lax.dynamic_index_in_dim(
        cur_list.reshape(total_rows, slot_pairs, grid_cols), col_index, axis=2, keepdims=False
    )
    candidates = residue_lists[inner_safe]
    matches = (
        (candidates[:, None, :, :] == out_cols[:, :, None, None])
        & valid_inner[:, None, :, None]
        & valid_out[:, :, None, None]
    )
    chosen = jnp.sum(matches * jnp.arange(slot_pairs, dtype=jnp.int32), axis=-1)
    present = jnp.any(matches, axis=-1)
    position = inner_safe[:, None, :] * slot_pairs + chosen
    picked = jnp.where(
        present[..., None, None], column_panels[position], jnp.zeros((), jnp.bfloat16)
    )
    product = jnp.einsum(
        "ikuv,ilkvw->iluw", gathered_rows, picked, preferred_element_type=jnp.float32
    )
    keep = (my_residue[:, None, :] == out_cols[:, :, None]) & valid_out[:, :, None]
    previous = jnp.sum(jnp.where(keep[..., None, None], owned_slots[:, None], 0.0), axis=2)
    updated = jnp.where(trace_now > occupied, product, 2.0 * previous - product)
    return (updated.reshape(block_rows, 1, slot_pairs, 1, edge_size, edge_size), next_trace)


def shards(pattern_in, pattern_mid, pattern_out, density_blocks):
    grid_rows = lax.axis_size("row")
    grid_cols = lax.axis_size("col")
    row_index = lax.axis_index("row")
    col_index = lax.axis_index("col")
    all_lists = (pattern_in, pattern_mid, pattern_out)
    current = density_blocks
    for iteration in range(ITERS):
        current, known_trace = purify_section(
            current,
            all_lists[iteration],
            all_lists[iteration + 1],
            grid_rows,
            grid_cols,
            row_index,
            col_index,
        )
    return current


def solution(mesh):
    in_specs = (P(), P(), P(), P(None, "row", None, "col", None, None))
    out_specs = P(None, "row", None, "col", None, None)
    return jax.shard_map(shards, mesh=mesh, in_specs=in_specs, out_specs=out_specs, check_vma=False)
```

profile of v0, /device:TPU:1, one launch (start us, length us, event | category | flops | bytes accessed | tf_op | source)
XLA Modules:
  0.0 392.0 jit_solution(4681731561013483844)
XLA Ops:
  6.5 2.8 convert_element_type.11
  9.4 0.0 all-gather.7.cloned.1.call-update
  9.4 0.0 all-gather.9.cloned.1.call-start
  9.5 0.7 all-gather.9.cloned.1.call-update
  10.2 0.0 all-gather.13.cloned.1.call-start
  10.2 1.8 copy.96
  12.0 0.1 reshape.153
  12.1 0.1 constant_dynamic-slice_fusion.5
  12.2 0.1 copy.128
  12.3 0.1 reshape.154
  12.4 0.1 constant_dynamic-slice_fusion.4
  12.5 0.1 copy.94
  12.6 0.1 copy.95
  12.7 1.9 fusion.9
  14.6 0.7 select_reduce_fusion.6
  15.3 72.1 %psum.14 = f32[]{:T(128)} all-reduce(f32[]{:T(128)} %select_reduce_fusion.6), channel_id=1, replica_groups=mesh['row'=16,'col'=8] {'row','col'}, use_global_device_ids=true, to_apply=%region_2.3 | all-reduce | flops 1 | bytes 8 | tf_op jit(solution)/shard_map/psum | solution.py:29
  87.5 0.1 reshape.151
  87.5 0.1 constant_dynamic-slice_fusion.7
  87.6 0.1 copy.127
  87.7 0.1 reshape.152
  87.8 0.2 compare_reduce_fusion.1
  88.0 0.1 copy.91
  88.1 0.1 reshape.159
  88.2 0.1 constant_dynamic-slice_fusion.1
  88.3 0.1 copy.131
  88.4 0.1 reshape.160
  88.5 0.2 compare_reduce_fusion
  88.7 0.1 copy.111
  88.8 0.1 reshape.166
  88.9 0.1 copy.98
  89.0 0.6 gather_fusion
  89.6 0.1 copy.124
  89.7 0.1 copy.92
  89.9 0.1 fusion.17
  90.0 0.1 reshape.174
  90.1 0.1 copy.116
  90.1 0.1 compare_and_fusion
  90.2 1.7 select_reduce_fusion.1
  92.0 2.0 copy.106
  94.6 30.6 %all-gather.7.cloned.1.call-done = bf16[4,16,2,1,256,256]{5,4,3,2,1,0:T(8,128)(2,1)} async-done(((bf16[4,1,2,1,256,256]{5,4,3,2,1,0:T(8,128)(2,1)}), bf16[4,16,2,1,256,256]{5,4,3,2,1,0:T(8,128)(2,1)}) %all-gather.7.cloned.1.call-update) | async-done | bytes 16777232 | tf_op jit(solution)/shard_map/all_gather | solution.py:42
  125.2 14.7 %gather_fusion.1 = bf16[128,256,256]{2,1,0:T(8,128)(2,1)} fusion(bf16[128,256,256]{2,1,0:T(8,128)(2,1)} %bitcast.85, s32[1024]{0:T(1024)S(1)} %pad_clamp_fusion.2), kind=kCustom, calls=%fused_computation.1 | custom fusion | bytes 33554944 | tf_op jit(solution)/shard_map/gather | solution.py:58
  139.8 21.8 %copy.102 = bf16[128,256,256]{1,2,0:T(8,128)(2,1)} copy(bf16[128,256,256]{2,1,0:T(8,128)(2,1)} %gather_fusion.1) | data formatting | bytes 33554432 | tf_op jit(solution)/shard_map/gather | solution.py:58
  161.6 15.0 %all-gather.9.cloned.1.call-done = bf16[4,1,2,8,256,256]{5,4,3,2,1,0:T(8,128)(2,1)} async-done(((bf16[4,1,2,1,256,256]{5,4,3,2,1,0:T(8,128)(2,1)}), bf16[4,1,2,8,256,256]{5,4,3,2,1,0:T(8,128)(2,1)}) %all-gather.9.cloned.1.call-update) | async-done | bytes 8388624 | tf_op jit(solution)/shard_map/all_gather | solution.py:30
  176.6 12.1 %select_reduce_fusion.2 = (f32[4,2]{1,0:T(4,128)S(1)}, bf16[4,2,256,256]{2,3,1,0:T(8,128)(2,1)}, f32[4,2,256,256]{2,3,1,0:T(8,128)}) fusion(pred[256,256]{0,1:T(8,128)(4,1)S(1)} %iota_compare_fusion, f32[4,2,256,256]{2,3,1,0:T(8,128)S(1)} %copy.106, bf16[4,16,256,256,1]{3,2,1,4,0:T(8,128)(2,1)} %bitcast.101, bf16[4,2,16,256,256]{3,4,2,1,0:T(8,128)(2,1)} %bitcast.87, ...), kind=kOutput, calls=%fused_computation.19 | convolution fusion | flops 4306501632 | bytes 30474400 | tf_op jit(solution)/shard_map/ikuv,ilkvw->iluw/dot_general | solution.py:60
  188.8 0.0 all-gather.13.cloned.1.call-update
  188.8 0.0 all-gather.11.cloned.1.call-start
  188.8 0.5 all-gather.11.cloned.1.call-update
  189.4 0.1 reshape.182
  189.4 0.1 copy.108
  189.5 0.6 gather_fusion.2
  190.1 0.1 copy.126
  190.2 0.1 fusion.16
  190.4 0.1 reshape.190
  190.5 0.8 select_reduce_fusion.5
  191.2 66.4 %psum.15 = f32[]{:T(128)} all-reduce(f32[]{:T(128)} %select_reduce_fusion.5), channel_id=1, replica_groups=mesh['row'=16,'col'=8] {'row','col'}, use_global_device_ids=true, to_apply=%region_8.9 | all-reduce | flops 1 | bytes 8 | tf_op jit(solution)/shard_map/psum | solution.py:29
  257.6 2.2 copy.117
  259.8 1.7 select_reduce_fusion
  261.5 1.9 copy.118
  264.1 0.0 all-gather.13.cloned.1.call-done
  264.2 11.5 %copy.114 = bf16[4,2,2048,256]{3,2,1,0:T(8,128)(2,1)} copy(bf16[4,2,2048,256]{2,3,1,0:T(8,128)(2,1)} %all-gather.13.cloned.1.call-done) | data formatting | bytes 16777216 | tf_op jit(solution)/shard_map/all_gather | solution.py:30
  275.7 81.2 %all-gather.11.cloned.1.call-done = bf16[4,32,256,256]{2,3,1,0:T(8,128)(2,1)} async-done(((bf16[4,2,256,256]{2,3,1,0:T(8,128)(2,1)}), bf16[4,32,256,256]{2,3,1,0:T(8,128)(2,1)}) %all-gather.11.cloned.1.call-update) | async-done | bytes 16777232 | tf_op jit(solution)/shard_map/all_gather | solution.py:42
  356.9 14.1 %gather_fusion.3 = bf16[128,256,256]{1,2,0:T(8,128)(2,1)} fusion(bf16[128,256,256]{1,2,0:T(8,128)(2,1)} %bitcast.86, s32[1024]{0:T(1024)S(1)} %pad_clamp_fusion), kind=kCustom, calls=%fused_computation.3 | custom fusion | bytes 33554944 | tf_op jit(solution)/shard_map/gather | solution.py:58
  371.0 11.6 %fusion.8 = f32[4,1,2,1,256,256]{4,5,2,0,3,1:T(8,128)} fusion(f32[4,2,256,256]{2,3,1,0:T(8,128)S(1)} %copy.118, bf16[4,16,256,256,1]{3,2,1,4,0:T(8,128)(2,1)} %bitcast.89, bf16[4,2,16,256,256]{3,4,2,1,0:T(8,128)(2,1)} %bitcast.88, pred[4,2,16]{2,1,0:T(4,128)(4,1)S(1)} %copy.112, pred[]{:T(512)S(6)} %gt.7), kind=kOutput, calls=%fused_computation.16 | convolution fusion | flops 4304928768 | bytes 29360256 | tf_op jit(solution)/shard_map/ikuv,ilkvw->iluw/dot_general | solution.py:60
  382.5 2.9 copy.119
  (25 shorter events, 0.2 us)
Async XLA Ops:
  6.5 3.7 copy-start
  6.5 5.5 %copy-start.2 = (s32[64,16]{0,1:T(8,128)S(1)}, s32[64,16]{0,1:T(8,128)}, u32[]{:S(2)}) copy-start(s32[64,16]{0,1:T(8,128)} %param.4) | copy-start | bytes 12292
  6.5 118.6 %all-gather.7.cloned.1.call-start = ((), (), s32[]{:S(2)}) async-start(), calls=%async_computation | async-start | bytes 17825792 | tf_op jit(solution)/shard_map/all_gather | solution.py:42
  9.4 78.1 %copy-start.1 = (s32[64,16]{0,1:T(8,128)S(1)}, s32[64,16]{0,1:T(8,128)}, u32[]{:S(2)}) copy-start(s32[64,16]{0,1:T(8,128)} %param.5) | copy-start | bytes 12292
  9.4 78.8 %copy-start.3 = (s32[64,16]{0,1:T(8,128)S(1)}, s32[64,16]{0,1:T(8,128)}, u32[]{:S(2)}) copy-start(s32[64,16]{0,1:T(8,128)} %param.6) | copy-start | bytes 12292
  9.4 167.2 %all-gather.9.cloned.1.call-start = ((), (), s32[]{:S(2)}) async-start(), calls=%async_computation.1 | async-start | bytes 9437184 | tf_op jit(solution)/shard_map/all_gather | solution.py:30
  10.2 254.0 %all-gather.13.cloned.1.call-start = ((), (), s32[]{:S(2)}) async-start(), calls=%async_computation.3 | async-start | bytes 9437184 | tf_op jit(solution)/shard_map/all_gather | solution.py:30
  188.8 168.1 %all-gather.11.cloned.1.call-start = ((), (), s32[]{:S(2)}) async-start(), calls=%async_computation.2 | async-start | bytes 17825792 | tf_op jit(solution)/shard_map/all_gather | solution.py:42
Sparse Core Ops, SparseCore 0:
  9.5 115.5 all-gather.6
  126.8 49.7 all-gather.8
  188.9 54.5 all-gather.12
  245.6 111.2 all-gather.10
where the time goes:
time: 393 us; the launch traced here: 392 us
  blocking collectives  139 us (35%)
  waiting for transfers between devices  128 us (33%)
  local copies, waits for them, and re-layouts  76.5 us (19%)
  matrix products  23.7 us (6%)
  between operations  14.5 us (4%)
  other arithmetic  10.5 us (3%)
    psum x2, blocking collectives, purify_section(): trace_now = lax.psum(diag_term, ('row', 'col'))  139 us
    all_gather x2, waiting for transfers between devices, purify_section(): lax.all_gather(panels, 'row', axis=1, tiled=True)  112 us
    gather x3, local copies, waits for them, and re-layouts, purify_section(): column_panels[position]  50.5 us
    dot_general x2, matrix products, purify_section(): jnp.einsum('ikuv,ilkvw->iluw', gathered_rows, picked, preferred_element_t...  23.7 us
    all_gather x2, waiting for transfers between devices, purify_section(): lax.all_gather(panels, 'col', axis=3, tiled=True)  15.1 us
    all_gather x1, local copies, waits for them, and re-layouts, purify_section(): lax.all_gather(panels, 'col', axis=3, tiled=True)  11.5 us
  transfers between devices with their start and end apart: 4, of which 3 were waited for; matrix products, arithmetic and copies ran while one was open for 17% of the time, Pallas kernels for 0%

commit v1 on v0

--- a/solution.py
+++ b/solution.py
@@ -4,6 +4,28 @@
 from jax.sharding import PartitionSpec as P
 
 ITERS = 2
+
+
+def laid_out(tiles, dim):
+    tiles = jnp.moveaxis(tiles, 0, dim)
+    shape = tiles.shape
+    return tiles.reshape(*shape[:dim], shape[dim] * shape[dim + 1], *shape[dim + 2 :])
+
+
+def ring_gather(x, axis, dim):
+    size = lax.axis_size(axis)
+    pairs = [(i, (i + 1) % size) for i in range(size)]
+    back = [(b, a) for a, b in pairs]
+    lower, upper = ([], [])
+    for lap in range(size - 1):
+        if lap % 2 == 0:
+            lower.append(lax.ppermute(lower[-1] if lower else x, axis, pairs))
+        else:
+            upper.append(lax.ppermute(upper[-1] if upper else x, axis, back))
+    blocks = jnp.stack([*lower[::-1], x, *upper])
+    shift = lax.axis_index(axis) - len(lower)
+    blocks = blocks[(jnp.arange(size) - shift) % size]
+    return laid_out(blocks, dim)
 
 
 def purify_section(owned, cur_list, next_list, grid_rows, grid_cols, row_index, col_index):
@@ -27,7 +49,7 @@
     )
     next_trace = None
     trace_now = lax.psum(diag_term, ("row", "col"))
-    gathered_rows = lax.all_gather(panels, "col", axis=3, tiled=True).reshape(
+    gathered_rows = ring_gather(panels, "col", 3).reshape(
         block_rows, slot_count, edge_size, edge_size
     )
     next_rows = lax.dynamic_index_in_dim(

time: 393 us -> 431 us (1.097)
  waiting for transfers between devices: 128 us -> 57.4 us
  local copies, waits for them, and re-layouts: 76.5 us -> 146 us
  starting transfers between devices: 0.12 us -> 24.3 us
  blocking collectives: 139 us -> 149 us
    all_gather x2, waiting for transfers between devices: 112 us -> 0.01 us  [purify_section(): lax.all_gather(panels, 'row', axis=1, tiled=True)]
    ppermute x0 -> x14, waiting for transfers between devices: none -> 57.3 us  [the longest x8 56.9 us: ring_gather(): lower.append(lax.ppermute(lower[-1] if lower else x, axis, pairs))]
    unnamed x12 -> x27, local copies, waits for them, and re-layouts: 2.14 us -> 29.5 us
    ppermute x0 -> x14, starting transfers between devices: none -> 24.3 us  [the longest x8 18.6 us: ring_gather(): lower.append(lax.ppermute(lower[-1] if lower else x, axis, pairs))]
    transpose x0 -> x2, local copies, waits for them, and re-layouts: none -> 19 us  [laid_out(): tiles = jnp.moveaxis(tiles, 0, dim)]
    gather x0 -> x2, local copies, waits for them, and re-layouts: none -> 16.1 us  [ring_gather(): blocks = blocks[(jnp.arange(size) - shift) % size]]
    all_gather x2 -> x0, waiting for transfers between devices: 15.1 us -> none  [purify_section(): lax.all_gather(panels, 'col', axis=3, tiled=True)]
    psum x2, blocking collectives: 139 us -> 149 us  [purify_section(): trace_now = lax.psum(diag_term, ('row', 'col'))]
  transfers between devices with their start and end apart: 4 -> 16, of which waited for: 3 -> 7; matrix products, arithmetic and copies ran while one was open for 17% -> 21% of each run, Pallas kernels for 0% -> 0%
where the time goes in v1:
time: 431 us; the launch traced here: 429 us
  blocking collectives  149 us (35%)
  local copies, waits for them, and re-layouts  146 us (34%)
  waiting for transfers between devices  57.4 us (13%)
  starting transfers between devices  24.3 us (6%)
  matrix products  23.6 us (5%)
  between operations  14.8 us (3%)
  other arithmetic  13.2 us (3%)
    psum x2, blocking collectives, purify_section(): trace_now = lax.psum(diag_term, ('row', 'col'))  149 us
    ppermute x8, waiting for transfers between devices, ring_gather(): lower.append(lax.ppermute(lower[-1] if lower else x, axis, pairs))  56.9 us
    gather x3, local copies, waits for them, and re-layouts, purify_section(): column_panels[position]  49.9 us
    unnamed x27, local copies, waits for them, and re-layouts  29.5 us
    dot_general x2, matrix products, purify_section(): jnp.einsum('ikuv,ilkvw->iluw', gathered_rows, picked, preferred_element_t...  23.6 us
    transpose x2, local copies, waits for them, and re-layouts, laid_out(): tiles = jnp.moveaxis(tiles, 0, dim)  19 us
    ppermute x8, starting transfers between devices, ring_gather(): lower.append(lax.ppermute(lower[-1] if lower else x, axis, pairs))  18.6 us
    gather x2, local copies, waits for them, and re-layouts, ring_gather(): blocks = blocks[(jnp.arange(size) - shift) % size]  16.1 us
  transfers between devices with their start and end apart: 16, of which 7 were waited for; matrix products, arithmetic and copies ran while one was open for 21% of the time, Pallas kernels for 0%

profile of v1, /device:TPU:1, one launch (start us, length us, event | category | flops | bytes accessed | tf_op | source)
XLA Modules:
  0.0 428.9 jit_solution(8795401166853029946)
XLA Ops:
  6.5 2.8 fusion.22
  9.5 1.7 bitcast_convert_fusion
  11.2 3.0 collective-permute-start
  14.2 0.8 reshape.202
  15.0 0.8 reshape.197
  15.8 10.1 %collective-permute-done = bf16[4,1,2,1,256,256]{5,4,2,0,3,1:T(8,128)(2,1)} collective-permute-done((bf16[4,1,2,1,256,256]{5,4,2,0,3,1:T(8,128)(2,1)S(1)}, bf16[4,1,2,1,256,256]{5,4,2,0,3,1:T(8,128)(2,1)}, u32[]{:S(2)}, u32[]{:S(2)}) %collective-permute-start) | collective-permute-done | bytes 1048608 | tf_op jit(solution)/shard_map/ppermute | solution.py:22
  25.9 2.6 collective-permute-start.1
  29.0 0.8 reshape.195
  30.1 0.7 constant_dynamic-slice_fusion.2
  31.4 9.2 %collective-permute-done.1 = bf16[4,1,2,1,256,256]{5,4,2,0,3,1:T(8,128)(2,1)} collective-permute-done((bf16[4,1,2,1,256,256]{5,4,2,0,3,1:T(8,128)(2,1)}, bf16[4,1,2,1,256,256]{5,4,2,0,3,1:T(8,128)(2,1)}, u32[]{:S(2)}, u32[]{:S(2)}) %collective-permute-start.1) | collective-permute-done | bytes 1048608 | tf_op jit(solution)/shard_map/ppermute | solution.py:22
  40.6 2.5 collective-permute-start.2
  43.1 1.8 copy.183
  46.1 1.9 fusion.9
  48.0 0.7 select_reduce_fusion.6
  48.8 1.5 collective-permute-start.5
  50.2 4.9 %collective-permute-done.2 = bf16[4,1,2,1,256,256]{5,4,2,0,3,1:T(8,128)(2,1)} collective-permute-done((bf16[4,1,2,1,256,256]{5,4,2,0,3,1:T(8,128)(2,1)}, bf16[4,1,2,1,256,256]{5,4,2,0,3,1:T(8,128)(2,1)}, u32[]{:S(2)}, u32[]{:S(2)}) %collective-permute-start.2) | collective-permute-done | bytes 1048608 | tf_op jit(solution)/shard_map/ppermute | solution.py:22
  55.1 2.5 collective-permute-start.3
  57.6 76.3 %psum.14 = f32[]{:T(128)} all-reduce(f32[]{:T(128)} %select_reduce_fusion.6), channel_id=1, replica_groups=mesh['row'=16,'col'=8] {'row','col'}, use_global_device_ids=true, to_apply=%region_2.3 | all-reduce | flops 1 | bytes 8 | tf_op jit(solution)/shard_map/psum | solution.py:51
  134.3 1.7 select_reduce_fusion.1
  136.0 2.9 copy.204
  139.6 1.2 collective-permute-start.6
  140.8 2.3 bitcast_dynamic-update-slice_fusion.6
  143.1 2.3 bitcast_dynamic-update-slice_fusion.5
  145.4 2.3 bitcast_dynamic-update-slice_fusion.4
  147.7 2.3 bitcast_dynamic-update-slice_fusion.3
  150.0 1.1 bitcast_dynamic-update-slice_fusion.2
  151.1 2.3 bitcast_dynamic-update-slice_fusion.1
  153.4 1.1 bitcast_dynamic-update-slice_fusion
  154.4 1.0 bitcast_dynamic-update-slice_fusion.15
  155.5 8.0 %gather_fusion.2 = bf16[8,4,2,256,256]{4,3,2,1,0:T(8,128)(2,1)} fusion(bf16[8,4,2,256,256]{4,3,2,1,0:T(8,128)(2,1)} %bitcast.28, s32[1024]{0:T(1024)S(1)} %pad_clamp_fusion.2), kind=kCustom, calls=%fused_computation.2 | custom fusion | bytes 16777248 | tf_op jit(solution)/shard_map/gather | solution.py:27
  163.5 7.6 %copy.200 = bf16[4,1,2,8,1,256,256]{6,5,3,2,0,4,1:T(8,128)(2,1)} copy(bf16[4,1,2,8,1,256,256]{6,5,2,0,3,4,1:T(8,128)(2,1)} %bitcast.153) | data formatting | bytes 16777216 | tf_op jit(solution)/shard_map/transpose | solution.py:10
  171.1 13.9 %copy.190 = bf16[4,16,2,1,256,256]{5,4,2,1,0,3:T(8,128)(2,1)} copy(bf16[4,16,2,1,256,256]{5,4,3,2,0,1:T(8,128)(2,1)} %all-gather.4.cloned.1.call-done) | data formatting | bytes 33554432 | tf_op jit(solution)/shard_map/all_gather | solution.py:64
  185.0 14.2 %gather_fusion.1 = bf16[128,256,256]{2,1,0:T(8,128)(2,1)} fusion(bf16[128,256,256]{2,1,0:T(8,128)(2,1)} %bitcast.149, s32[1024]{0:T(1024)S(1)} %pad_clamp_fusion.3), kind=kCustom, calls=%fused_computation.1 | custom fusion | bytes 33554944 | tf_op jit(solution)/shard_map/gather | solution.py:80
  199.2 21.7 %copy.192 = bf16[4,2,16,256,256]{3,4,2,1,0:T(8,128)(2,1)} copy(bf16[4,2,16,256,256]{4,3,2,1,0:T(8,128)(2,1)} %bitcast.150) | data formatting | bytes 33554432 | tf_op jit(solution)/shard_map/gather | solution.py:80
  220.8 12.1 %select_reduce_fusion.2 = (f32[4,2]{1,0:T(4,128)S(1)}, bf16[4,2,256,256]{2,3,1,0:T(8,128)(2,1)}, f32[4,2,256,256]{2,3,1,0:T(8,128)}) fusion(pred[256,256]{0,1:T(8,128)(4,1)S(1)} %iota_compare_fusion, f32[4,2,256,256]{2,3,1,0:T(8,128)S(1)} %copy-done.2, bf16[4,16,256,256,1]{3,2,1,4,0:T(8,128)(2,1)} %bitcast.156, bf16[4,2,16,256,256]{3,4,2,1,0:T(8,128)(2,1)} %copy.192, ...), kind=kOutput, calls=%fused_computation.22 | convolution fusion | flops 4306501632 | bytes 30474400 | tf_op jit(solution)/shard_map/ikuv,ilkvw->iluw/dot_general | solution.py:82
  233.0 0.6 collective-permute-start.7
  233.6 12.1 %collective-permute-done.7 = bf16[4,1,2,1,256,256]{4,5,2,0,3,1:T(8,128)(2,1)S(1)} collective-permute-done((bf16[4,1,2,1,256,256]{4,5,2,0,3,1:T(8,128)(2,1)}, bf16[4,1,2,1,256,256]{4,5,2,0,3,1:T(8,128)(2,1)S(1)}, u32[]{:S(2)}, u32[]{:S(2)}) %collective-permute-start.7) | collective-permute-done | bytes 1048608 | tf_op jit(solution)/shard_map/ppermute | solution.py:22
  245.6 2.4 collective-permute-start.8
  248.0 0.7 collective-permute-start.11
  248.7 11.0 %collective-permute-done.8 = bf16[4,1,2,1,256,256]{4,5,2,0,3,1:T(8,128)(2,1)S(1)} collective-permute-done((bf16[4,1,2,1,256,256]{4,5,2,0,3,1:T(8,128)(2,1)S(1)}, bf16[4,1,2,1,256,256]{4,5,2,0,3,1:T(8,128)(2,1)S(1)}, u32[]{:S(2)}, u32[]{:S(2)}) %collective-permute-start.8) | collective-permute-done | bytes 1048608 | tf_op jit(solution)/shard_map/ppermute | solution.py:22
  259.7 2.5 collective-permute-start.9
  262.7 1.6 collective-permute-start.12
  264.3 9.7 %collective-permute-done.9 = bf16[4,1,2,1,256,256]{4,5,2,0,3,1:T(8,128)(2,1)} collective-permute-done((bf16[4,1,2,1,256,256]{4,5,2,0,3,1:T(8,128)(2,1)S(1)}, bf16[4,1,2,1,256,256]{4,5,2,0,3,1:T(8,128)(2,1)}, u32[]{:S(2)}, u32[]{:S(2)}) %collective-permute-start.9) | collective-permute-done | bytes 1048608 | tf_op jit(solution)/shard_map/ppermute | solution.py:22
  274.0 2.6 collective-permute-start.10
  276.7 0.6 gather_fusion.3
  277.6 0.7 select_reduce_fusion.5
  278.2 73.0 %psum.15 = f32[]{:T(128)} all-reduce(f32[]{:T(128)} %select_reduce_fusion.5), channel_id=1, replica_groups=mesh['row'=16,'col'=8] {'row','col'}, use_global_device_ids=true, to_apply=%region_8.9 | all-reduce | flops 1 | bytes 8 | tf_op jit(solution)/shard_map/psum | solution.py:51
  351.8 1.9 copy.215
  353.8 1.7 select_reduce_fusion
  355.5 1.9 copy.216
  357.4 0.7 collective-permute-start.13
  358.2 2.3 bitcast_dynamic-update-slice_fusion.14
  360.5 2.3 bitcast_dynamic-update-slice_fusion.13
  362.8 2.3 bitcast_dynamic-update-slice_fusion.12
  365.1 2.3 bitcast_dynamic-update-slice_fusion.11
  367.4 1.0 bitcast_dynamic-update-slice_fusion.10
  368.4 2.3 bitcast_dynamic-update-slice_fusion.9
  370.7 2.3 bitcast_dynamic-update-slice_fusion.8
  373.0 1.1 bitcast_dynamic-update-slice_fusion.7
  374.1 8.0 %gather_fusion.5 = bf16[8,4,2,256,256]{3,4,2,1,0:T(8,128)(2,1)} fusion(bf16[8,4,2,256,256]{3,4,2,1,0:T(8,128)(2,1)} %bitcast.58, s32[1024]{0:T(1024)S(1)} %pad_clamp_fusion.2), kind=kCustom, calls=%fused_computation.5 | custom fusion | bytes 16777248 | tf_op jit(solution)/shard_map/gather | solution.py:27
  382.1 11.5 %copy.212 = bf16[4,1,2,8,1,256,256]{6,5,3,2,0,4,1:T(8,128)(2,1)} copy(bf16[4,1,2,8,1,256,256]{5,6,2,0,3,4,1:T(8,128)(2,1)} %bitcast.152) | data formatting | bytes 16777216 | tf_op jit(solution)/shard_map/transpose | solution.py:10
  393.6 14.1 %gather_fusion.4 = bf16[128,256,256]{1,2,0:T(8,128)(2,1)} fusion(bf16[128,256,256]{1,2,0:T(8,128)(2,1)} %bitcast.154, s32[1024]{0:T(1024)S(1)} %pad_clamp_fusion), kind=kCustom, calls=%fused_computation.4 | custom fusion | bytes 33554944 | tf_op jit(solution)/shard_map/gather | solution.py:80
  407.6 11.6 %fusion.8 = f32[4,1,2,1,256,256]{4,5,2,0,3,1:T(8,128)} fusion(f32[4,2,256,256]{2,3,1,0:T(8,128)S(1)} %copy.216, bf16[4,16,256,256,1]{3,2,1,4,0:T(8,128)(2,1)} %bitcast.157, bf16[4,2,16,256,256]{3,4,2,1,0:T(8,128)(2,1)} %bitcast.155, pred[4,2,16]{2,1,0:T(4,128)(4,1)S(1)} %copy.210, pred[]{:T(512)S(6)} %gt.7), kind=kOutput, calls=%fused_computation.18 | convolution fusion | flops 4304928768 | bytes 29360256 | tf_op jit(solution)/shard_map/ikuv,ilkvw->iluw/dot_general | solution.py:82
  419.2 2.9 copy.217
  (72 shorter events, 4.1 us)
Async XLA Ops:
  6.5 36.5 %copy-start = (f32[4,1,2,1,256,256]{5,4,3,2,1,0:T(8,128)S(1)}, f32[4,1,2,1,256,256]{5,4,3,2,1,0:T(8,128)}, u32[]{:S(2)}) copy-start(f32[4,1,2,1,256,256]{5,4,3,2,1,0:T(8,128)} %param.7) | copy-start | bytes 6291460
  6.5 164.6 %all-gather.4.cloned.1.call-start = ((), (), s32[]{:S(2)}) async-start(), calls=%async_computation | async-start | bytes 17825792 | tf_op jit(solution)/shard_map/all_gather | solution.py:64
  9.4 384.2 %all-gather.6.cloned.1.call-start = ((), (), s32[]{:S(2)}) async-start(), calls=%async_computation.1 | async-start | bytes 17825792 | tf_op jit(solution)/shard_map/all_gather | solution.py:64
  11.2 14.8 %collective-permute-start = (bf16[4,1,2,1,256,256]{5,4,2,0,3,1:T(8,128)(2,1)S(1)}, bf16[4,1,2,1,256,256]{5,4,2,0,3,1:T(8,128)(2,1)}, u32[]{:S(2)}, u32[]{:S(2)}) collective-permute-start(bf16[4,1,2,1,256,256]{5,4,2,0,3,1:T(8,128)(2,1)S(1)} %bitcast_convert_fusion), channel_id=1, source_target_pairs={{0,1},{1,2},{2,3},{3,4},{4,5},{5,6},{6,7},{7,0},{8,9},{9,10},{10,1... | collective-permute-start | bytes 3145736 | tf_op jit(solution)/shard_map/ppermute | solution.py:22
  14.2 34.6 %collective-permute-start.4 = (bf16[4,1,2,1,256,256]{5,4,2,0,3,1:T(8,128)(2,1)S(1)}, bf16[4,1,2,1,256,256]{5,4,2,0,3,1:T(8,128)(2,1)}, u32[]{:S(2)}, u32[]{:S(2)}) collective-permute-start(bf16[4,1,2,1,256,256]{5,4,2,0,3,1:T(8,128)(2,1)S(1)} %bitcast_convert_fusion), channel_id=1, source_target_pairs={{1,0},{2,1},{3,2},{4,3},{5,4},{6,5},{7,6},{0,7},{9,8},{10,9},{11,1... | collective-permute-start | bytes 3145736 | tf_op jit(solution)/shard_map/ppermute | solution.py:24
  25.9 14.6 %collective-permute-start.1 = (bf16[4,1,2,1,256,256]{5,4,2,0,3,1:T(8,128)(2,1)}, bf16[4,1,2,1,256,256]{5,4,2,0,3,1:T(8,128)(2,1)}, u32[]{:S(2)}, u32[]{:S(2)}) collective-permute-start(bf16[4,1,2,1,256,256]{5,4,2,0,3,1:T(8,128)(2,1)} %collective-permute-done), channel_id=1, source_target_pairs={{0,1},{1,2},{2,3},{3,4},{4,5},{5,6},{6,7},{7,0},{8,9},{9,10},{10,1... | collective-permute-start | bytes 3145736 | tf_op jit(solution)/shard_map/ppermute | solution.py:22
  40.6 14.5 %collective-permute-start.2 = (bf16[4,1,2,1,256,256]{5,4,2,0,3,1:T(8,128)(2,1)}, bf16[4,1,2,1,256,256]{5,4,2,0,3,1:T(8,128)(2,1)}, u32[]{:S(2)}, u32[]{:S(2)}) collective-permute-start(bf16[4,1,2,1,256,256]{5,4,2,0,3,1:T(8,128)(2,1)} %collective-permute-done.1), channel_id=1, source_target_pairs={{0,1},{1,2},{2,3},{3,4},{4,5},{5,6},{6,7},{7,0},{8,9},{9,10},{10,1... | collective-permute-start | bytes 3145736 | tf_op jit(solution)/shard_map/ppermute | solution.py:22
  48.8 90.9 %collective-permute-start.5 = (bf16[4,1,2,1,256,256]{5,4,2,0,3,1:T(8,128)(2,1)}, bf16[4,1,2,1,256,256]{5,4,2,0,3,1:T(8,128)(2,1)S(1)}, u32[]{:S(2)}, u32[]{:S(2)}) collective-permute-start(bf16[4,1,2,1,256,256]{5,4,2,0,3,1:T(8,128)(2,1)} %collective-permute-done.4), channel_id=1, source_target_pairs={{1,0},{2,1},{3,2},{4,3},{5,4},{6,5},{7,6},{0,7},{9,8},{10,9},{11,1... | collective-permute-start | bytes 3145736 | tf_op jit(solution)/shard_map/ppermute | solution.py:24
  55.1 85.7 %collective-permute-start.3 = (bf16[4,1,2,1,256,256]{5,4,2,0,3,1:T(8,128)(2,1)}, bf16[4,1,2,1,256,256]{5,4,2,0,3,1:T(8,128)(2,1)}, u32[]{:S(2)}, u32[]{:S(2)}) collective-permute-start(bf16[4,1,2,1,256,256]{5,4,2,0,3,1:T(8,128)(2,1)} %collective-permute-done.2), channel_id=1, source_target_pairs={{0,1},{1,2},{2,3},{3,4},{4,5},{5,6},{6,7},{7,0},{8,9},{9,10},{10,1... | collective-permute-start | bytes 3145736 | tf_op jit(solution)/shard_map/ppermute | solution.py:22
  139.6 14.8 %collective-permute-start.6 = (bf16[4,1,2,1,256,256]{5,4,2,0,3,1:T(8,128)(2,1)S(1)}, bf16[4,1,2,1,256,256]{5,4,2,0,3,1:T(8,128)(2,1)S(1)}, u32[]{:S(2)}, u32[]{:S(2)}) collective-permute-start(bf16[4,1,2,1,256,256]{5,4,2,0,3,1:T(8,128)(2,1)S(1)} %collective-permute-done.5), channel_id=1, source_target_pairs={{1,0},{2,1},{3,2},{4,3},{5,4},{6,5},{7,6},{0,7},{9,8},{10,9},{11,1... | collective-permute-start | bytes 3145736 | tf_op jit(solution)/shard_map/ppermute | solution.py:24
  199.2 21.7 %copy-start.2 = (f32[4,2,256,256]{2,3,1,0:T(8,128)S(1)}, f32[4,2,256,256]{2,3,1,0:T(8,128)}, u32[]{:S(2)}) copy-start(f32[4,2,256,256]{2,3,1,0:T(8,128)} %copy.204) | copy-start | bytes 6291460
  233.0 12.7 %collective-permute-start.7 = (bf16[4,1,2,1,256,256]{4,5,2,0,3,1:T(8,128)(2,1)}, bf16[4,1,2,1,256,256]{4,5,2,0,3,1:T(8,128)(2,1)S(1)}, u32[]{:S(2)}, u32[]{:S(2)}) collective-permute-start(bf16[4,1,2,1,256,256]{4,5,2,0,3,1:T(8,128)(2,1)} %bitcast.158), channel_id=1, source_target_pairs={{0,1},{1,2},{2,3},{3,4},{4,5},{5,6},{6,7},{7,0},{8,9},{9,10},{10,1... | collective-permute-start | bytes 3145736 | tf_op jit(solution)/shard_map/ppermute | solution.py:22
  245.6 30.9 %copy-start.3 = (bf16[4,1,2,1,256,256]{4,5,2,0,3,1:T(8,128)(2,1)}, bf16[4,1,2,1,256,256]{4,5,2,0,3,1:T(8,128)(2,1)S(1)}, u32[]{:S(2)}) copy-start(bf16[4,1,2,1,256,256]{4,5,2,0,3,1:T(8,128)(2,1)S(1)} %collective-permute-done.7) | copy-start | bytes 3145732
  245.6 14.1 %collective-permute-start.8 = (bf16[4,1,2,1,256,256]{4,5,2,0,3,1:T(8,128)(2,1)S(1)}, bf16[4,1,2,1,256,256]{4,5,2,0,3,1:T(8,128)(2,1)S(1)}, u32[]{:S(2)}, u32[]{:S(2)}) collective-permute-start(bf16[4,1,2,1,256,256]{4,5,2,0,3,1:T(8,128)(2,1)S(1)} %collective-permute-done.7), channel_id=1, source_target_pairs={{0,1},{1,2},{2,3},{3,4},{4,5},{5,6},{6,7},{7,0},{8,9},{9,10},{10,1... | collective-permute-start | bytes 3145736 | tf_op jit(solution)/shard_map/ppermute | solution.py:22
  248.0 14.7 %collective-permute-start.11 = (bf16[4,1,2,1,256,256]{4,5,2,0,3,1:T(8,128)(2,1)}, bf16[4,1,2,1,256,256]{4,5,2,0,3,1:T(8,128)(2,1)}, u32[]{:S(2)}, u32[]{:S(2)}) collective-permute-start(bf16[4,1,2,1,256,256]{4,5,2,0,3,1:T(8,128)(2,1)} %bitcast.159), channel_id=1, source_target_pairs={{1,0},{2,1},{3,2},{4,3},{5,4},{6,5},{7,6},{0,7},{9,8},{10,9},{11,1... | collective-permute-start | bytes 3145736 | tf_op jit(solution)/shard_map/ppermute | solution.py:24
  259.7 92.1 %copy-start.4 = (bf16[4,1,2,1,256,256]{4,5,2,0,3,1:T(8,128)(2,1)}, bf16[4,1,2,1,256,256]{4,5,2,0,3,1:T(8,128)(2,1)S(1)}, u32[]{:S(2)}) copy-start(bf16[4,1,2,1,256,256]{4,5,2,0,3,1:T(8,128)(2,1)S(1)} %collective-permute-done.8) | copy-start | bytes 3145732
  259.7 14.2 %collective-permute-start.9 = (bf16[4,1,2,1,256,256]{4,5,2,0,3,1:T(8,128)(2,1)S(1)}, bf16[4,1,2,1,256,256]{4,5,2,0,3,1:T(8,128)(2,1)}, u32[]{:S(2)}, u32[]{:S(2)}) collective-permute-start(bf16[4,1,2,1,256,256]{4,5,2,0,3,1:T(8,128)(2,1)S(1)} %collective-permute-done.8), channel_id=1, source_target_pairs={{0,1},{1,2},{2,3},{3,4},{4,5},{5,6},{6,7},{7,0},{8,9},{9,10},{10,1... | collective-permute-start | bytes 3145736 | tf_op jit(solution)/shard_map/ppermute | solution.py:22
  262.7 94.7 %collective-permute-start.12 = (bf16[4,1,2,1,256,256]{4,5,2,0,3,1:T(8,128)(2,1)}, bf16[4,1,2,1,256,256]{4,5,2,0,3,1:T(8,128)(2,1)}, u32[]{:S(2)}, u32[]{:S(2)}) collective-permute-start(bf16[4,1,2,1,256,256]{4,5,2,0,3,1:T(8,128)(2,1)} %collective-permute-done.11), channel_id=1, source_target_pairs={{1,0},{2,1},{3,2},{4,3},{5,4},{6,5},{7,6},{0,7},{9,8},{10,9},{11,1... | collective-permute-start | bytes 3145736 | tf_op jit(solution)/shard_map/ppermute | solution.py:24
  274.0 84.2 %collective-permute-start.10 = (bf16[4,1,2,1,256,256]{4,5,2,0,3,1:T(8,128)(2,1)}, bf16[4,1,2,1,256,256]{4,5,2,0,3,1:T(8,128)(2,1)}, u32[]{:S(2)}, u32[]{:S(2)}) collective-permute-start(bf16[4,1,2,1,256,256]{4,5,2,0,3,1:T(8,128)(2,1)} %collective-permute-done.9), channel_id=1, source_target_pairs={{0,1},{1,2},{2,3},{3,4},{4,5},{5,6},{6,7},{7,0},{8,9},{9,10},{10,1... | collective-permute-start | bytes 3145736 | tf_op jit(solution)/shard_map/ppermute | solution.py:22
  353.8 13.6 %copy-start.1 = (bf16[4,2,256,256]{2,3,1,0:T(8,128)(2,1)S(1)}, bf16[4,2,256,256]{2,3,1,0:T(8,128)(2,1)}, u32[]{:S(2)}) copy-start(bf16[4,2,256,256]{2,3,1,0:T(8,128)(2,1)} %get-tuple-element.14) | copy-start | bytes 3145732
  357.4 15.6 %collective-permute-start.13 = (bf16[4,1,2,1,256,256]{4,5,2,0,3,1:T(8,128)(2,1)}, bf16[4,1,2,1,256,256]{4,5,2,0,3,1:T(8,128)(2,1)S(1)}, u32[]{:S(2)}, u32[]{:S(2)}) collective-permute-start(bf16[4,1,2,1,256,256]{4,5,2,0,3,1:T(8,128)(2,1)} %collective-permute-done.12), channel_id=1, source_target_pairs={{1,0},{2,1},{3,2},{4,3},{5,4},{6,5},{7,6},{0,7},{9,8},{10,9},{11,1... | collective-permute-start | bytes 3145736 | tf_op jit(solution)/shard_map/ppermute | solution.py:24
Sparse Core Ops, SparseCore 0:
  9.5 115.4 all-gather.3
  233.1 109.0 all-gather.5
